TPU v7x, 256 devices: a whole 4x4x8 slice. The times are simulated.
256 devices in a mesh: ctx: 16 (over z, core), tp: 16 (over x, y).
Axes of the slice: x: 4, y: 4, z: 8, core: 2. Of those that a mesh axis runs over, the one named last changes fastest.
Arguments:
- q_act: bfloat16 [64, 128, 4096], P('ctx', None, 'tp'), may hold values from -16 to 16
- k_act: bfloat16 [64, 128, 4096], P('ctx', None, 'tp'), may hold values from -16 to 16
- v_act: bfloat16 [64, 128, 4096], P('ctx', None, 'tp'), may hold values from -6 to 6
- grad_out: bfloat16 [8192, 4096], P(('ctx', 'tp')), may hold values from -24 to 24
- w_out: bfloat16 [4096, 4096], P(None, 'tp'), may hold values from -0.09375 to 0.09375
- nbr_tiles: int32 [64, 12], replicated, may hold values from 0 to 63, as said below
- nbr_valid: int32 [64, 12], replicated, may hold values from 0 to 1, as said below
- slot_of: int32 [64], replicated, may hold values from 0 to 63, as said below
Outputs:
- grad_q: bfloat16 [64, 128, 4096], P('ctx', None, 'tp')
- grad_k: bfloat16 [64, 128, 4096], P('ctx', None, 'tp')
- grad_v: bfloat16 [64, 128, 4096], P('ctx', None, 'tp')
- grad_w_out: bfloat16 [4096, 4096], P('ctx', 'tp')
Inputs may be any that keep to these rules, and one draw needn't show every extreme that they name: `nbr_tiles`: row t lists scenario tiles linked to tile t; the live entries of a row name distinct tiles, one of them t itself. `nbr_valid`: every row has at least one live entry; a tile is named by live entries of at most 12 rows. `slot_of`: a permutation; slots c * 4 to c * 4 + 3 are held by index c of ctx.
All inputs are finite; a program needn't handle non-finite values.
Results may differ from a plain program's by a relative error of at most 0.024.
Values may be sent and summed in bfloat16 or wider, within the bound.
No kernel may reach another device: no remote copies, remote signals or barrier semaphores. Data moves between devices by JAX's collectives and lax.ppermute only.
A program may use at most 128 MiB of HBM per device.

v0:
```python
import math
import jax
import jax.numpy as jnp
from jax import lax
from jax.sharding import Mesh
from jax.sharding import PartitionSpec as P

HD = 128
CORES = 2


def slot_tables(nbr_tiles, nbr_valid, slot_of):
    tile_count = slot_of.shape[0]
    slot_index = jnp.arange(tile_count, dtype=jnp.int32)
    matches = (slot_of[:, None] == slot_index[None, :]).astype(jnp.int32)
    near_tiles = jnp.einsum("ts,tj->sj", matches, nbr_tiles)
    live_mask = jnp.einsum("ts,tj->sj", matches, nbr_valid)
    found = (near_tiles[:, :, None] == slot_index[None, None, :]).astype(jnp.int32)
    key_slot = jnp.sum(found * slot_of[None, None, :], axis=2)
    return (key_slot, live_mask)


def to_head(arrays, local_tiles, tile_len, heads_here):
    stacked = jnp.stack([a.reshape(local_tiles, tile_len, heads_here, HD) for a in arrays], axis=1)
    moved = lax.all_to_all(stacked, "core", split_axis=3, concat_axis=0, tiled=True)
    return moved.reshape(local_tiles * heads_here, len(arrays), tile_len, HD)


def from_head(arrays, local_tiles, tile_len, heads_here):
    stacked = jnp.stack(arrays, axis=1)[:, :, :, None, :]
    moved = lax.all_to_all(stacked, "core", split_axis=0, concat_axis=3, tiled=True)
    return tuple(
        (moved[:, n].reshape(local_tiles, tile_len, heads_here * HD) for n in range(len(arrays)))
    )


def ring_gather(x, axis, count):
    ahead = [(i, (i - 1) % count) for i in range(count)]
    behind = [(i, (i + 1) % count) for i in range(count)]
    half = count // 2
    later = [x]
    earlier = []
    down = x
    up = x
    for _ in range(1, half):
        down = lax.ppermute(down, axis, ahead)
        up = lax.ppermute(up, axis, behind)
        later.append(down)
        earlier.append(up)
    if count % 2 == 0 and count > 1:
        cut = x.shape[0] // 2
        first = lax.ppermute(up[:cut], axis, behind)
        second = lax.ppermute(down[cut:], axis, ahead)
        later.append(jnp.concatenate([first, second], axis=0))
    return jnp.concatenate(later + earlier[::-1], axis=0)


def ring_index(slots, own, chip_tiles, count):
    return (slots // chip_tiles - own) % count * chip_tiles + slots % chip_tiles


def per_device(q_act, k_act, v_act, grad_out, w_out, nbr_tiles, nbr_valid, slot_of):
    local_tiles, tile_len, col_width = q_act.shape
    heads_here = col_width // HD
    score_scale = 1.0 / math.sqrt(HD)
    chip_tiles = local_tiles * heads_here
    z_count = lax.axis_size("z")
    own_z = lax.axis_index("z")
    first_slot = own_z * chip_tiles
    key_slot, live_mask = slot_tables(nbr_tiles, nbr_valid, slot_of)
    tile_count = key_slot.shape[0]
    list_len = key_slot.shape[1]
    near_slots = lax.dynamic_slice_in_dim(key_slot, first_slot, chip_tiles, 0)
    near_live = lax.dynamic_slice_in_dim(live_mask, first_slot, chip_tiles, 0)
    full_rows = lax.all_gather(grad_out, "tp", axis=0, tiled=True)
    grad_flat = jnp.dot(full_rows, w_out, preferred_element_type=jnp.float32).astype(jnp.bfloat16)
    grad_tiles = grad_flat.reshape(local_tiles, tile_len, col_width)
    head_parts = to_head((k_act, v_act, q_act), local_tiles, tile_len, heads_here)
    key_h = head_parts[:, 0]
    value_h = head_parts[:, 1]
    query_h = head_parts[:, 2]
    grad_h = to_head((grad_tiles,), local_tiles, tile_len, heads_here)[:, 0]
    kv_all = ring_gather(head_parts[:, 0:2], "z", z_count)
    near_index = ring_index(near_slots.reshape(-1), own_z, chip_tiles, z_count)
    near = kv_all[near_index].reshape(chip_tiles, list_len, 2, tile_len, HD)
    near_keys = near[:, :, 0].reshape(chip_tiles, list_len * tile_len, HD)
    near_values = near[:, :, 1].reshape(chip_tiles, list_len * tile_len, HD)
    live_cells = jnp.repeat(near_live > 0, tile_len, axis=1)[:, None, :]
    scores = (
        jnp.einsum("sad,sbd->sab", query_h, near_keys, preferred_element_type=jnp.float32)
        * score_scale
    )
    row_peak = jnp.max(jnp.where(live_cells, scores, -1e30), axis=2, keepdims=True)
    row_total = jnp.sum(
        jnp.where(live_cells, jnp.exp(scores - row_peak), 0.0), axis=2, keepdims=True
    )
    log_total = row_peak + jnp.log(row_total)
    prob_full = jnp.where(live_cells, jnp.exp(scores - log_total), 0.0)
    prob_half = prob_full.astype(jnp.bfloat16)
    attn_h = jnp.einsum(
        "sab,sbd->sad", prob_half, near_values, preferred_element_type=jnp.float32
    ).astype(jnp.bfloat16)
    row_delta = jnp.einsum("sad,sad->sa", grad_h, attn_h, preferred_element_type=jnp.float32)
    grad_prob = jnp.einsum("sad,sbd->sab", grad_h, near_values, preferred_element_type=jnp.float32)
    grad_score = (prob_full * (grad_prob - row_delta[:, :, None])).astype(jnp.bfloat16)
    grad_query_h = (
        jnp.einsum("sab,sbd->sad", grad_score, near_keys, preferred_element_type=jnp.float32)
        * score_scale
    ).astype(jnp.bfloat16)
    attn_tiles, grad_q = from_head((attn_h, grad_query_h), local_tiles, tile_len, heads_here)
    qg_all = lax.all_gather(jnp.stack([query_h, grad_h], axis=1), "z", axis=0, tiled=True)
    stats_all = lax.all_gather(
        jnp.stack([log_total[:, :, 0], row_delta], axis=1), "z", axis=0, tiled=True
    )
    owned_slots = first_slot + jnp.arange(chip_tiles, dtype=jnp.int32)
    pair_hits = (key_slot[:, :, None] == owned_slots[None, None, :]) & (live_mask[:, :, None] > 0)
    named_by = jnp.any(pair_hits, axis=1).astype(jnp.int32)
    rank_of = jnp.cumsum(named_by, axis=0) - 1
    list_pos = jnp.arange(list_len, dtype=jnp.int32)
    placed = (named_by[:, :, None] > 0) & (rank_of[:, :, None] == list_pos[None, None, :])
    slot_index = jnp.arange(tile_count, dtype=jnp.int32)
    picked = jnp.sum(placed.astype(jnp.int32) * slot_index[:, None, None], axis=0)
    picked_live = jnp.any(placed, axis=0)
    picked_index = picked.reshape(-1)
    rows = qg_all[picked_index].reshape(chip_tiles, list_len, 2, tile_len, HD)
    query_rows = rows[:, :, 0].reshape(chip_tiles, list_len * tile_len, HD)
    grad_rows = rows[:, :, 1].reshape(chip_tiles, list_len * tile_len, HD)
    stat_rows = stats_all[picked_index].reshape(chip_tiles, list_len, 2, tile_len)
    total_rows = stat_rows[:, :, 0].reshape(chip_tiles, 1, list_len * tile_len)
    delta_rows = stat_rows[:, :, 1].reshape(chip_tiles, 1, list_len * tile_len)
    keep_pair = jnp.repeat(picked_live, tile_len, axis=1)[:, None, :]
    owner_scores = (
        jnp.einsum("tbd,tad->tba", key_h, query_rows, preferred_element_type=jnp.float32)
        * score_scale
    )
    owner_probs = jnp.where(keep_pair, jnp.exp(owner_scores - total_rows), 0.0)
    owner_grad_prob = jnp.einsum(
        "tbd,tad->tba", value_h, grad_rows, preferred_element_type=jnp.float32
    )
    owner_grad_score = (owner_probs * (owner_grad_prob - delta_rows)).astype(jnp.bfloat16)
    grad_key_h = (
        jnp.einsum("tba,tad->tbd", owner_grad_score, query_rows, preferred_element_type=jnp.float32)
        * score_scale
    ).astype(jnp.bfloat16)
    grad_value_h = jnp.einsum(
        "tba,tad->tbd",
        owner_probs.astype(jnp.bfloat16),
        grad_rows,
        preferred_element_type=jnp.float32,
    ).astype(jnp.bfloat16)
    grad_k, grad_v = from_head((grad_key_h, grad_value_h), local_tiles, tile_len, heads_here)
    attn_flat = attn_tiles.reshape(local_tiles * tile_len, col_width)
    weight_part = lax.dot_general(
        full_rows, attn_flat, (((0,), (0,)), ((), ())), preferred_element_type=jnp.float32
    )
    model_width = weight_part.shape[0]
    block_rows = model_width // (z_count * CORES)
    by_core = weight_part.reshape(z_count, CORES, block_rows, col_width).transpose(1, 0, 2, 3)
    chip_sum = lax.psum_scatter(by_core, "core", scatter_dimension=0, tiled=True)
    grad_weight = lax.psum_scatter(
        chip_sum.reshape(z_count * block_rows, col_width).astype(jnp.bfloat16),
        "z",
        scatter_dimension=0,
        tiled=True,
    )
    return (grad_q, grad_k, grad_v, grad_weight)


def solution(mesh):
    ctx_count = mesh.shape["ctx"]
    tp_count = mesh.shape["tp"]
    devices = mesh.devices.reshape(ctx_count // CORES, CORES, tp_count)
    chip_mesh = Mesh(devices, ("z", "core", "tp"))
    tiles = ("z", "core")
    in_specs = (
        P(tiles, None, "tp"),
        P(tiles, None, "tp"),
        P(tiles, None, "tp"),
        P((*tiles, "tp"), None),
        P(None, "tp"),
        P(),
        P(),
        P(),
    )
    out_specs = (P(tiles, None, "tp"), P(tiles, None, "tp"), P(tiles, None, "tp"), P(tiles, "tp"))
    return jax.shard_map(
        per_device, mesh=chip_mesh, in_specs=in_specs, out_specs=out_specs, check_vma=False
    )
```

profile of v0, /device:TPU:4, one launch (start us, length us, event | category | flops | bytes accessed | tf_op | source)
XLA Modules:
  0.0 305.9 jit_solution(6664586194276471653)
XLA Ops:
  7.2 0.7 all-gather.3.cloned.1.call-update
  8.0 1.1 copy.62
  9.1 1.1 copy.61
  10.2 1.8 copy.60
  12.0 1.0 pad_maximum_fusion
  13.0 1.2 copy.63
  14.2 5.4 %all_to_all.66 = bf16[4,3,128,2,128]{4,2,0,1,3:T(8,128)(2,1)S(1)} all-to-all(bf16[4,3,128,2,128]{4,2,0,1,3:T(8,128)(2,1)} %copy.63), channel_id=1, replica_groups=mesh['z'=8,'core'=2,'tp'=16] {'core'}, dimensions={3} | all-to-all | bytes 1572864 | tf_op jit(solution)/shard_map/all_to_all | solution.py:25
  19.8 50.1 %all-gather.3.cloned.1.call-done = bf16[512,4096]{1,0:T(8,128)(2,1)} async-done(((bf16[32,4096]{1,0:T(8,128)(2,1)}), bf16[512,4096]{1,0:T(8,128)(2,1)}) %all-gather.3.cloned.1.call-update) | async-done | bytes 4194320 | tf_op jit(solution)/shard_map/all_gather | solution.py:75
  69.8 3.4 %convolution_convert_fusion = bf16[512,256]{1,0:T(8,128)(2,1)S(1)} fusion(bf16[512,4096]{1,0:T(8,128)(2,1)} %all-gather.3.cloned.1.call-done, bf16[4096,256]{1,0:T(8,128)(2,1)S(1)} %copy-done), kind=kOutput, calls=%fused_computation.29 | convolution fusion | flops 1073872896 | bytes 6553600 | tf_op jit(solution)/shard_map/dot_general | solution.py:76
  73.4 3.9 %all_to_all.67 = bf16[4,1,128,2,128]{4,2,0,1,3:T(8,128)(2,1)S(1)} all-to-all(bf16[4,1,128,2,128]{4,2,0,1,3:T(8,128)(2,1)S(1)} %copy.67), channel_id=1, replica_groups=mesh['z'=8,'core'=2,'tp'=16] {'core'}, dimensions={3} | all-to-all | bytes 524288 | tf_op jit(solution)/shard_map/all_to_all | solution.py:25
  77.3 0.8 pad_maximum_fusion.1
  78.3 1.1 fusion.59
  79.3 3.3 %collective-permute-start = (bf16[8,2,128,128]{3,2,0,1:T(8,128)(2,1)S(1)}, bf16[8,2,128,128]{3,2,0,1:T(8,128)(2,1)S(1)}, u32[]{:S(2)}, u32[]{:S(2)}) collective-permute-start(bf16[8,2,128,128]{3,2,0,1:T(8,128)(2,1)S(1)} %get-tuple-element.10), channel_id=1, source_target_pairs={{0,224},{32,0},{64,32},{96,64},{128,96},{160,128},{192,160},{224,1... | collective-permute-start | bytes 1572872 | tf_op jit(solution)/shard_map/ppermute | solution.py:46
  82.6 0.2 fusion.39
  82.8 0.4 select_reduce_fusion.2
  83.5 16.3 %collective-permute-done = bf16[8,2,128,128]{3,2,0,1:T(8,128)(2,1)S(1)} collective-permute-done((bf16[8,2,128,128]{3,2,0,1:T(8,128)(2,1)S(1)}, bf16[8,2,128,128]{3,2,0,1:T(8,128)(2,1)S(1)}, u32[]{:S(2)}, u32[]{:S(2)}) %collective-permute-start) | collective-permute-done | bytes 524320 | tf_op jit(solution)/shard_map/ppermute | solution.py:46
  99.8 3.7 %collective-permute-start.1 = (bf16[8,2,128,128]{3,2,0,1:T(8,128)(2,1)S(1)}, bf16[8,2,128,128]{3,2,0,1:T(8,128)(2,1)S(1)}, u32[]{:S(2)}, u32[]{:S(2)}) collective-permute-start(bf16[8,2,128,128]{3,2,0,1:T(8,128)(2,1)S(1)} %collective-permute-done), channel_id=1, source_target_pairs={{0,224},{32,0},{64,32},{96,64},{128,96},{160,128},{192,160},{224,1... | collective-permute-start | bytes 1572872 | tf_op jit(solution)/shard_map/ppermute | solution.py:46
  103.6 0.2 broadcast_compare_fusion
  103.8 25.9 %collective-permute-done.4 = bf16[8,2,128,128]{3,2,0,1:T(8,128)(2,1)S(1)} collective-permute-done((bf16[8,2,128,128]{3,2,0,1:T(8,128)(2,1)S(1)}, bf16[8,2,128,128]{3,2,0,1:T(8,128)(2,1)S(1)}, u32[]{:S(2)}, u32[]{:S(2)}) %collective-permute-start.4) | collective-permute-done | bytes 524320 | tf_op jit(solution)/shard_map/ppermute | solution.py:47
  129.7 3.3 %collective-permute-start.2 = (bf16[8,2,128,128]{3,2,0,1:T(8,128)(2,1)S(1)}, bf16[8,2,128,128]{3,2,0,1:T(8,128)(2,1)S(1)}, u32[]{:S(2)}, u32[]{:S(2)}) collective-permute-start(bf16[8,2,128,128]{3,2,0,1:T(8,128)(2,1)S(1)} %collective-permute-done.1), channel_id=1, source_target_pairs={{0,224},{32,0},{64,32},{96,64},{128,96},{160,128},{192,160},{224,1... | collective-permute-start | bytes 1572872 | tf_op jit(solution)/shard_map/ppermute | solution.py:46
  133.1 22.4 %collective-permute-done.5 = bf16[8,2,128,128]{3,2,0,1:T(8,128)(2,1)S(1)} collective-permute-done((bf16[8,2,128,128]{3,2,0,1:T(8,128)(2,1)S(1)}, bf16[8,2,128,128]{3,2,0,1:T(8,128)(2,1)S(1)}, u32[]{:S(2)}, u32[]{:S(2)}) %collective-permute-start.5) | collective-permute-done | bytes 524320 | tf_op jit(solution)/shard_map/ppermute | solution.py:47
  155.7 1.9 constant_dynamic-update-slice_fusion.7
  157.6 3.5 %collective-permute-start.7 = (bf16[4,2,128,128]{3,2,0,1:T(8,128)(2,1)S(1)}, bf16[4,2,128,128]{3,2,0,1:T(8,128)(2,1)S(1)}, u32[]{:S(2)}, u32[]{:S(2)}) collective-permute-start(bf16[4,2,128,128]{3,2,0,1:T(8,128)(2,1)S(1)} %slice.73), channel_id=1, source_target_pairs={{0,224},{32,0},{64,32},{96,64},{128,96},{160,128},{192,160},{224,1... | collective-permute-start | bytes 786440 | tf_op jit(solution)/shard_map/ppermute | solution.py:53
  161.1 0.9 constant_dynamic-update-slice_fusion.6
  162.0 0.9 constant_dynamic-update-slice_fusion.5
  162.9 2.0 collective-permute-done.6
  164.9 0.8 constant_dynamic-update-slice_fusion.4
  165.7 0.7 constant_dynamic-update-slice_fusion.3
  166.4 0.9 constant_dynamic-update-slice_fusion.2
  167.3 0.9 constant_dynamic-update-slice_fusion.1
  168.2 0.9 constant_dynamic-update-slice_fusion
  169.1 8.2 %gather_fusion = bf16[96,2,128,128]{3,2,1,0:T(8,128)(2,1)} fusion(bf16[64,2,128,128]{3,2,0,1:T(8,128)(2,1)} %constant_dynamic-update-slice_fusion, s32[1024]{0:T(1024)S(1)} %pad_clamp_fusion.1), kind=kCustom, calls=%fused_computation | custom fusion | bytes 12583296 | tf_op jit(solution)/shard_map/gather | solution.py:85
  177.3 4.2 %fusion.58 = (bf16[8,12,1,128,128]{4,3,2,1,0:T(8,128)(2,1)S(1)}, bf16[8,12,1,128,128]{4,3,2,1,0:T(8,128)(2,1)S(1)}) fusion(bf16[8,12,2,128,128]{4,3,2,1,0:T(8,128)(2,1)} %bitcast.106), kind=kLoop, calls=%fused_computation.110 | loop fusion | bytes 12582912 | tf_op jit(solution)/shard_map/slice | solution.py:87
  181.6 1.1 select_reduce_fusion.1
  182.7 0.5 copy-done.3
  183.2 1.5 select_reduce_fusion
  184.7 1.7 fusion.31
  186.4 7.4 %fusion.27 = bf16[8,1,128,128]{3,2,0,1:T(8,128)(2,1)S(1)} fusion(bf16[8,1536,128]{2,1,0:T(8,128)(2,1)} %bitcast.112, f32[8,128,1536]{2,1,0:T(8,128)} %copy-done.2, bf16[8,128,128]{2,1,0:T(8,128)(2,1)S(1)} %bitcast.129, bf16[8,1536,128]{2,1,0:T(8,128)(2,1)} %bitcast.123, f32[8,128]{1,0:T(8,128)S(1)} %get-tuple-element.20, f32[8,128]{1,0:T(8,128)S(1)} %log_add_fusion, ...), kind=kOutput, calls=%fused_computation.32 | convolution fusion | flops 815005696 | bytes 13127680 | tf_op jit(solution)/shard_map/sab,sbd->sad/dot_general | solution.py:107
  193.9 4.4 %all_to_all.68 = bf16[8,2,128,1,128]{4,2,1,3,0:T(8,128)(2,1)S(1)} all-to-all(bf16[8,2,128,1,128]{4,2,1,3,0:T(8,128)(2,1)S(1)} %copy.68), channel_id=1, replica_groups=mesh['z'=8,'core'=2,'tp'=16] {'core'}, dimensions={0} | all-to-all | bytes 1048576 | tf_op jit(solution)/shard_map/all_to_all | solution.py:31
  198.3 0.5 copy.93
  198.8 0.4 fusion.60
  199.2 3.4 %convolution_bitcast_fusion = f32[4096,256]{0,1:T(8,128)} fusion(bf16[512,4096]{1,0:T(8,128)(2,1)S(1)} %copy-done.4, bf16[64,8,2,128]{3,2,1,0:T(2,128)(2,1)S(1)} %bitcast.127), kind=kOutput, calls=%fused_computation.9 | convolution fusion | flops 1073741824 | bytes 8650752 | tf_op jit(solution)/shard_map/dot_general | solution.py:153
  202.6 6.6 %reshape.268 = f32[8,2,256,256]{2,1,0,3:T(2,128)} reshape(f32[4096,256]{0,1:T(8,128)} %convolution_bitcast_fusion) | data formatting | bytes 8388608 | tf_op jit(solution)/shard_map/reshape | solution.py:158
  209.2 7.2 %copy.76 = f32[8,2,256,256]{3,2,0,1:T(8,128)} copy(f32[8,2,256,256]{2,1,0,3:T(2,128)} %reshape.268) | data formatting | bytes 8388608 | tf_op jit(solution)/shard_map/reshape | solution.py:158
  216.7 0.1 reduce_window_sum.11
  216.9 0.3 select_reduce_fusion.3
  217.3 0.3 fusion.38
  217.7 0.9 reshape_squeeze.25
  218.6 24.6 %all_gather.11 = f32[64,2,128]{2,1,0:T(2,128)S(1)} all-gather(f32[8,2,128]{2,1,0:T(2,128)S(1)} %pad_maximum_fusion.2), channel_id=1, replica_groups=mesh['z'=8,'core'=2,'tp'=16] {'z'}, dimensions={0}, use_global_device_ids=true | all-gather | bytes 73728 | tf_op jit(solution)/shard_map/all_gather | solution.py:112
  243.2 0.7 gather_fusion.2
  243.9 0.2 slice_reduce_fusion
  244.2 8.2 %gather_fusion.1 = bf16[96,2,128,128]{3,2,1,0:T(8,128)(2,1)} fusion(bf16[64,2,128,128]{3,2,0,1:T(8,128)(2,1)} %all-gather.5.cloned.1.call-done, s32[1024]{0:T(1024)S(1)} %pad_clamp_fusion), kind=kCustom, calls=%fused_computation.1 | custom fusion | bytes 12583296 | tf_op jit(solution)/shard_map/gather | solution.py:125
  252.4 8.1 %fusion.57 = (bf16[8,12,1,128,128]{4,3,2,1,0:T(8,128)(2,1)}, bf16[8,12,1,128,128]{4,3,2,1,0:T(8,128)(2,1)}) fusion(bf16[8,12,2,128,128]{4,3,2,1,0:T(8,128)(2,1)} %bitcast.107), kind=kLoop, calls=%fused_computation.109 | loop fusion | bytes 12582912 | tf_op jit(solution)/shard_map/slice | solution.py:126
  260.5 2.7 convert_element_type.57
  263.2 3.0 fusion.34
  266.3 1.3 fusion.28
  267.6 1.3 copy-done.5
  268.9 7.6 %fusion.26 = bf16[8,1,128,128]{3,2,0,1:T(8,128)(2,1)S(1)} fusion(bf16[8,1536,128]{2,1,0:T(8,128)(2,1)} %bitcast.110, f32[8,128,1536]{2,1,0:T(8,128)} %copy-done.5, bf16[8,1536,128]{2,1,0:T(8,128)(2,1)} %bitcast.120, f32[8,1536]{1,0:T(8,128)S(1)} %get-tuple-element.24, f32[8,1536]{1,0:T(8,128)S(1)} %get-tuple-element.25, ...), kind=kOutput, calls=%fused_computation.31 | convolution fusion | flops 815005696 | bytes 13217792 | tf_op jit(solution)/shard_map/tba,tad->tbd/dot_general | solution.py:142
  276.6 4.2 %all_to_all.69 = bf16[8,2,128,1,128]{4,2,1,3,0:T(8,128)(2,1)S(1)} all-to-all(bf16[8,2,128,1,128]{4,2,1,3,0:T(8,128)(2,1)S(1)} %copy.73), channel_id=1, replica_groups=mesh['z'=8,'core'=2,'tp'=16] {'core'}, dimensions={0} | all-to-all | bytes 1048576 | tf_op jit(solution)/shard_map/all_to_all | solution.py:31
  280.8 0.3 copy.74
  281.1 0.9 reshape_squeeze.28
  282.0 0.3 copy.75
  282.2 0.9 reshape_squeeze.29
  283.1 16.3 %reduce-scatter.5.cloned.1.call-done = bf16[256,256]{1,0:T(8,128)(2,1)} async-done(((bf16[2048,256]{1,0:T(8,128)(2,1)}), bf16[256,256]{1,0:T(8,128)(2,1)}) %reduce-scatter.5.cloned.1.call-update) | async-done | bytes 131088 | tf_op jit(solution)/shard_map/reduce_scatter | solution.py:160
  (71 shorter events, 1.8 us)
Async XLA Ops:
  7.2 62.6 %copy-start = (bf16[4096,256]{1,0:T(8,128)(2,1)S(1)}, bf16[4096,256]{1,0:T(8,128)(2,1)}, u32[]{:S(2)}) copy-start(bf16[4096,256]{1,0:T(8,128)(2,1)} %param.12) | copy-start | bytes 6291460
  7.2 62.6 %all-gather.3.cloned.1.call-start = ((), (), s32[]{:S(2)}) async-start(), calls=%async_computation.6 | async-start | bytes 4456448 | tf_op jit(solution)/shard_map/all_gather | solution.py:75
  7.9 236.3 %all-gather.5.cloned.1.call-start = ((), (), s32[]{:S(2)}) async-start(), calls=%async_computation.7 | async-start | bytes 4718592 | tf_op jit(solution)/shard_map/all_gather | solution.py:111
  73.2 9.4 %copy-start.9 = (s32[64]{0:T(128)S(1)}, s32[64]{0:T(128)}, u32[]{:S(2)}) copy-start(s32[64]{0:T(128)} %param.15) | copy-start | bytes 772
  73.3 9.4 %copy-start.10 = (s32[64,12]{0,1:T(8,128)S(1)}, s32[64,12]{0,1:T(8,128)}, u32[]{:S(2)}) copy-start(s32[64,12]{0,1:T(8,128)} %param.13) | copy-start | bytes 9220
  73.3 30.3 %copy-start.11 = (s32[64,12]{0,1:T(8,128)S(1)}, s32[64,12]{0,1:T(8,128)}, u32[]{:S(2)}) copy-start(s32[64,12]{0,1:T(8,128)} %param.14) | copy-start | bytes 9220
  78.2 182.3 %reduce-scatter.3.cloned.1.call-start = ((), (), s32[]{:S(2)}) async-start(), calls=%async_computation.8 | async-start | bytes 6291456 | tf_op jit(solution)/shard_map/reduce_scatter | solution.py:159
  79.3 20.5 %collective-permute-start = (bf16[8,2,128,128]{3,2,0,1:T(8,128)(2,1)S(1)}, bf16[8,2,128,128]{3,2,0,1:T(8,128)(2,1)S(1)}, u32[]{:S(2)}, u32[]{:S(2)}) collective-permute-start(bf16[8,2,128,128]{3,2,0,1:T(8,128)(2,1)S(1)} %get-tuple-element.10), channel_id=1, source_target_pairs={{0,224},{32,0},{64,32},{96,64},{128,96},{160,128},{192,160},{224,1... | collective-permute-start | bytes 1572872 | tf_op jit(solution)/shard_map/ppermute | solution.py:46
  82.6 20.9 %collective-permute-start.3 = (bf16[8,2,128,128]{3,2,0,1:T(8,128)(2,1)S(1)}, bf16[8,2,128,128]{3,2,0,1:T(8,128)(2,1)S(1)}, u32[]{:S(2)}, u32[]{:S(2)}) collective-permute-start(bf16[8,2,128,128]{3,2,0,1:T(8,128)(2,1)S(1)} %get-tuple-element.10), channel_id=1, source_target_pairs={{0,32},{32,64},{64,96},{96,128},{128,160},{160,192},{192,224},{224... | collective-permute-start | bytes 1572872 | tf_op jit(solution)/shard_map/ppermute | solution.py:47
  99.8 29.9 %copy-start.8 = (bf16[8,2,128,128]{3,2,0,1:T(8,128)(2,1)}, bf16[8,2,128,128]{3,2,0,1:T(8,128)(2,1)S(1)}, u32[]{:S(2)}) copy-start(bf16[8,2,128,128]{3,2,0,1:T(8,128)(2,1)S(1)} %collective-permute-done) | copy-start | bytes 1572868
  99.8 29.9 %collective-permute-start.1 = (bf16[8,2,128,128]{3,2,0,1:T(8,128)(2,1)S(1)}, bf16[8,2,128,128]{3,2,0,1:T(8,128)(2,1)S(1)}, u32[]{:S(2)}, u32[]{:S(2)}) collective-permute-start(bf16[8,2,128,128]{3,2,0,1:T(8,128)(2,1)S(1)} %collective-permute-done), channel_id=1, source_target_pairs={{0,224},{32,0},{64,32},{96,64},{128,96},{160,128},{192,160},{224,1... | collective-permute-start | bytes 1572872 | tf_op jit(solution)/shard_map/ppermute | solution.py:46
  103.5 26.1 %collective-permute-start.4 = (bf16[8,2,128,128]{3,2,0,1:T(8,128)(2,1)S(1)}, bf16[8,2,128,128]{3,2,0,1:T(8,128)(2,1)S(1)}, u32[]{:S(2)}, u32[]{:S(2)}) collective-permute-start(bf16[8,2,128,128]{3,2,0,1:T(8,128)(2,1)S(1)} %collective-permute-done.3), channel_id=1, source_target_pairs={{0,32},{32,64},{64,96},{96,128},{128,160},{160,192},{192,224},{224... | collective-permute-start | bytes 1572872 | tf_op jit(solution)/shard_map/ppermute | solution.py:47
  129.7 25.9 %collective-permute-start.5 = (bf16[8,2,128,128]{3,2,0,1:T(8,128)(2,1)S(1)}, bf16[8,2,128,128]{3,2,0,1:T(8,128)(2,1)S(1)}, u32[]{:S(2)}, u32[]{:S(2)}) collective-permute-start(bf16[8,2,128,128]{3,2,0,1:T(8,128)(2,1)S(1)} %collective-permute-done.4), channel_id=1, source_target_pairs={{0,32},{32,64},{64,96},{96,128},{128,160},{160,192},{192,224},{224... | collective-permute-start | bytes 1572872 | tf_op jit(solution)/shard_map/ppermute | solution.py:47
  129.7 27.9 %collective-permute-start.2 = (bf16[8,2,128,128]{3,2,0,1:T(8,128)(2,1)S(1)}, bf16[8,2,128,128]{3,2,0,1:T(8,128)(2,1)S(1)}, u32[]{:S(2)}, u32[]{:S(2)}) collective-permute-start(bf16[8,2,128,128]{3,2,0,1:T(8,128)(2,1)S(1)} %collective-permute-done.1), channel_id=1, source_target_pairs={{0,224},{32,0},{64,32},{96,64},{128,96},{160,128},{192,160},{224,1... | collective-permute-start | bytes 1572872 | tf_op jit(solution)/shard_map/ppermute | solution.py:46
  155.6 9.4 %collective-permute-start.6 = (bf16[4,2,128,128]{3,2,0,1:T(8,128)(2,1)S(1)}, bf16[4,2,128,128]{3,2,0,1:T(8,128)(2,1)S(1)}, u32[]{:S(2)}, u32[]{:S(2)}) collective-permute-start(bf16[4,2,128,128]{3,2,0,1:T(8,128)(2,1)S(1)} %slice.72), channel_id=1, source_target_pairs={{0,32},{32,64},{64,96},{96,128},{128,160},{160,192},{192,224},{224... | collective-permute-start | bytes 786440 | tf_op jit(solution)/shard_map/ppermute | solution.py:52
  157.6 8.1 %collective-permute-start.7 = (bf16[4,2,128,128]{3,2,0,1:T(8,128)(2,1)S(1)}, bf16[4,2,128,128]{3,2,0,1:T(8,128)(2,1)S(1)}, u32[]{:S(2)}, u32[]{:S(2)}) collective-permute-start(bf16[4,2,128,128]{3,2,0,1:T(8,128)(2,1)S(1)} %slice.73), channel_id=1, source_target_pairs={{0,224},{32,0},{64,32},{96,64},{128,96},{160,128},{192,160},{224,1... | collective-permute-start | bytes 786440 | tf_op jit(solution)/shard_map/ppermute | solution.py:53
  181.6 1.6 copy-start.3
  181.6 3.1 %copy-start.7 = (bf16[8,12,1,128,128]{4,3,2,1,0:T(8,128)(2,1)}, bf16[8,12,1,128,128]{4,3,2,1,0:T(8,128)(2,1)S(1)}, u32[]{:S(2)}) copy-start(bf16[8,12,1,128,128]{4,3,2,1,0:T(8,128)(2,1)S(1)} %get-tuple-element.8) | copy-start | bytes 9437188
  183.2 3.2 %copy-start.2 = (f32[8,128,1536]{2,1,0:T(8,128)}, f32[8,128,1536]{2,1,0:T(8,128)S(1)}, u32[]{:S(2)}) copy-start(f32[8,128,1536]{2,1,0:T(8,128)S(1)} %get-tuple-element.19) | copy-start | bytes 18874372
  193.8 5.5 %copy-start.4 = (bf16[512,4096]{1,0:T(8,128)(2,1)S(1)}, bf16[512,4096]{1,0:T(8,128)(2,1)}, u32[]{:S(2)}) copy-start(bf16[512,4096]{1,0:T(8,128)(2,1)} %all-gather.3.cloned.1.call-done) | copy-start | bytes 12582916
  216.5 82.9 %reduce-scatter.5.cloned.1.call-start = ((), (), s32[]{:S(2)}) async-start(), calls=%async_computation.9 | async-start | bytes 1179648 | tf_op jit(solution)/shard_map/reduce_scatter | solution.py:160
  263.2 3.0 copy-start.6
  266.2 2.7 copy-start.5
  268.9 30.5 %copy-start.1 = (bf16[4096,256]{1,0:T(8,128)(2,1)S(1)}, bf16[4096,256]{1,0:T(8,128)(2,1)}, u32[]{:S(2)}) copy-start(bf16[4096,256]{1,0:T(8,128)(2,1)} %param.12) | copy-start | bytes 6291460
Sparse Core Ops, SparseCore 0:
  10.4 59.3 all-gather.2
  78.3 83.5 all-gather.4
  216.6 14.3 reduce-scatter.2
  263.3 35.9 reduce-scatter.4
where the time goes:
time: 307 us; the launch traced here: 306 us
  waiting for transfers between devices  134 us (44%)
  local copies, waits for them, and re-layouts  64.6 us (21%)
  blocking collectives  42.6 us (14%)
  matrix products  29.3 us (10%)
  between operations  14.2 us (5%)
  starting transfers between devices  14 us (5%)
  other arithmetic  7.47 us (2%)
    all_gather x1, waiting for transfers between devices, per_device(): full_rows = lax.all_gather(grad_out, 'tp', axis=0, tiled=True)  50.1 us
    ppermute x3, waiting for transfers between devices, ring_gather(): up = lax.ppermute(up, axis, behind)  48.3 us
    all_gather x1, blocking collectives, per_device(): lax.all_gather(jnp.stack([log_total[:, :, 0], row_delta], axis=1), 'z', a...  24.6 us
    ppermute x3, waiting for transfers between devices, ring_gather(): down = lax.ppermute(down, axis, ahead)  16.3 us
    reduce_scatter x1, waiting for transfers between devices, per_device(): lax.psum_scatter(chip_sum.reshape(z_count * block_rows, col_width).astype...  16.3 us
    reshape x2, local copies, waits for them, and re-layouts, per_device(): weight_part.reshape(z_count, CORES, block_rows, col_width)  13.8 us
    unnamed x34, local copies, waits for them, and re-layouts  12.9 us
    ppermute x3, starting transfers between devices, ring_gather(): down = lax.ppermute(down, axis, ahead)  10.3 us
  transfers between devices with their start and end apart: 12, of which 6 were waited for; matrix products, arithmetic and copies ran while one was open for 30% of the time, Pallas kernels for 0%

commit v1 on v0

--- a/solution.py
+++ b/solution.py
@@ -60,6 +60,15 @@
 
 
 def per_device(q_act, k_act, v_act, grad_out, w_out, nbr_tiles, nbr_valid, slot_of):
+
+    def launch_the_bands(named_axis, row_data):
+        arrivals = []
+        for _ in range(jax.lax.axis_size(named_axis)):
+            arrivals.append(row_data)
+        val2 = jnp.stack(arrivals, axis=0)
+        new = jax.lax.all_to_all(val2, axis_name=named_axis, split_axis=0, concat_axis=0)
+        return jnp.concatenate(new, axis=0)
+
     local_tiles, tile_len, col_width = q_act.shape
     heads_here = col_width // HD
     score_scale = 1.0 / math.sqrt(HD)
@@ -72,7 +81,7 @@
     list_len = key_slot.shape[1]
     near_slots = lax.dynamic_slice_in_dim(key_slot, first_slot, chip_tiles, 0)
     near_live = lax.dynamic_slice_in_dim(live_mask, first_slot, chip_tiles, 0)
-    full_rows = lax.all_gather(grad_out, "tp", axis=0, tiled=True)
+    full_rows = launch_the_bands("tp", grad_out)
     grad_flat = jnp.dot(full_rows, w_out, preferred_element_type=jnp.float32).astype(jnp.bfloat16)
     grad_tiles = grad_flat.reshape(local_tiles, tile_len, col_width)
     head_parts = to_head((k_act, v_act, q_act), local_tiles, tile_len, heads_here)

time: 307 us -> 341 us (1.11)
  waiting for transfers between devices: 134 us -> 149 us
  starting transfers between devices: 14 us -> 24 us
  local copies, waits for them, and re-layouts: 64.6 us -> 69.5 us
    all_to_all x0 -> x1, waiting for transfers between devices: none -> 59.4 us  [launch_the_bands(): jax.lax.all_to_all(val2, axis_name=named_axis, split_axis=0, concat_axis=0)]
    all_gather x1 -> x0, waiting for transfers between devices: 50.1 us -> none  [per_device(): full_rows = lax.all_gather(grad_out, 'tp', axis=0, tiled=True)]
    all_to_all x0 -> x1, starting transfers between devices: none -> 7.45 us  [launch_the_bands(): jax.lax.all_to_all(val2, axis_name=named_axis, split_axis=0, concat_axis=0)]
    ppermute x3, waiting for transfers between devices: 16.3 us -> 10.6 us  [ring_gather(): down = lax.ppermute(down, axis, ahead)]
    reduce_scatter x1, waiting for transfers between devices: 16.3 us -> 21.9 us  [per_device(): lax.psum_scatter(chip_sum.reshape(z_count * block_rows, col_width).astype...]
    ppermute x1, waiting for transfers between devices: 2.02 us -> 7.42 us  [ring_gather(): first = lax.ppermute(up[:cut], axis, behind)]
    unnamed x34 -> x32, local copies, waits for them, and re-layouts: 12.9 us -> 13.1 us
  transfers between devices with their start and end apart: 12 -> 12, of which waited for: 6 -> 6; matrix products, arithmetic and copies ran while one was open for 30% -> 26% of each run, Pallas kernels for 0% -> 0%
where the time goes in v1:
time: 341 us; the launch traced here: 340 us
  waiting for transfers between devices  149 us (44%)
  local copies, waits for them, and re-layouts  69.5 us (20%)
  blocking collectives  43.2 us (13%)
  matrix products  31.3 us (9%)
  starting transfers between devices  24 us (7%)
  between operations  15.9 us (5%)
  other arithmetic  7.47 us (2%)
    all_to_all x1, waiting for transfers between devices, launch_the_bands(): jax.lax.all_to_all(val2, axis_name=named_axis, split_axis=0, concat_axis=0)  59.4 us
    ppermute x3, waiting for transfers between devices, ring_gather(): up = lax.ppermute(up, axis, behind)  49.3 us
    all_gather x1, blocking collectives, per_device(): lax.all_gather(jnp.stack([log_total[:, :, 0], row_delta], axis=1), 'z', a...  24.6 us
    reduce_scatter x1, waiting for transfers between devices, per_device(): lax.psum_scatter(chip_sum.reshape(z_count * block_rows, col_width).astype...  21.9 us
    reshape x2, local copies, waits for them, and re-layouts, per_device(): weight_part.reshape(z_count, CORES, block_rows, col_width)  13.8 us
    unnamed x32, local copies, waits for them, and re-layouts  13.1 us
    ppermute x3, starting transfers between devices, ring_gather(): down = lax.ppermute(down, axis, ahead)  12.9 us
    ppermute x3, waiting for transfers between devices, ring_gather(): down = lax.ppermute(down, axis, ahead)  10.6 us
  transfers between devices with their start and end apart: 12, of which 6 were waited for; matrix products, arithmetic and copies ran while one was open for 26% of the time, Pallas kernels for 0%

profile of v1, /device:TPU:4, one launch (start us, length us, event | category | flops | bytes accessed | tf_op | source)
XLA Modules:
  0.0 339.9 jit_solution(13576622672115894553)
XLA Ops:
  8.0 1.3 copy.62
  9.3 1.1 copy.61
  10.4 1.8 copy.60
  12.2 1.0 pad_maximum_fusion
  13.2 1.2 copy.63
  14.4 6.3 %all_to_all.71 = bf16[4,3,128,2,128]{4,2,0,1,3:T(8,128)(2,1)} all-to-all(bf16[4,3,128,2,128]{4,2,0,1,3:T(8,128)(2,1)} %copy.63), channel_id=1, replica_groups=mesh['z'=8,'core'=2,'tp'=16] {'core'}, dimensions={3} | all-to-all | bytes 1572864 | tf_op jit(solution)/shard_map/all_to_all | solution.py:25
  20.8 3.4 stack.24
  24.2 7.5 %all-to-all-start.1 = ((bf16[16,32,4096]{2,1,0:T(8,128)(2,1)}), bf16[16,32,4096]{2,1,0:T(8,128)(2,1)}, u32[]{:S(2)}, u32[]{:S(2)}) async-start(bf16[16,32,4096]{2,1,0:T(8,128)(2,1)} %stack.24), calls=%async_computation.1 | async-start | bytes 8388608 | tf_op jit(solution)/shard_map/all_to_all | solution.py:69
  31.7 1.2 copy.64
  32.9 59.4 %all-to-all-done.1 = bf16[16,32,4096]{2,1,0:T(8,128)(2,1)} async-done(((bf16[16,32,4096]{2,1,0:T(8,128)(2,1)}), bf16[16,32,4096]{2,1,0:T(8,128)(2,1)}, u32[]{:S(2)}, u32[]{:S(2)}) %all-to-all-start.1) | async-done | bytes 4194336 | tf_op jit(solution)/shard_map/all_to_all | solution.py:69
  92.3 3.4 %convolution_convert_fusion = bf16[512,256]{1,0:T(8,128)(2,1)S(1)} fusion(bf16[512,4096]{1,0:T(8,128)(2,1)} %bitcast.13, bf16[4096,256]{1,0:T(8,128)(2,1)S(1)} %copy-done), kind=kOutput, calls=%fused_computation.29 | convolution fusion | flops 1073872896 | bytes 6553600 | tf_op jit(solution)/shard_map/dot_general | solution.py:85
  95.9 3.9 %all_to_all.72 = bf16[4,1,128,2,128]{4,2,0,1,3:T(8,128)(2,1)S(1)} all-to-all(bf16[4,1,128,2,128]{4,2,0,1,3:T(8,128)(2,1)S(1)} %copy.67), channel_id=1, replica_groups=mesh['z'=8,'core'=2,'tp'=16] {'core'}, dimensions={3} | all-to-all | bytes 524288 | tf_op jit(solution)/shard_map/all_to_all | solution.py:25
  99.8 0.8 pad_maximum_fusion.1
  100.8 1.1 fusion.59
  101.8 5.9 %collective-permute-start = (bf16[8,2,128,128]{3,2,0,1:T(8,128)(2,1)S(1)}, bf16[8,2,128,128]{3,2,0,1:T(8,128)(2,1)S(1)}, u32[]{:S(2)}, u32[]{:S(2)}) collective-permute-start(bf16[8,2,128,128]{3,2,0,1:T(8,128)(2,1)S(1)} %get-tuple-element.10), channel_id=1, source_target_pairs={{0,224},{32,0},{64,32},{96,64},{128,96},{160,128},{192,160},{224,1... | collective-permute-start | bytes 1572872 | tf_op jit(solution)/shard_map/ppermute | solution.py:46
  107.9 0.4 select_reduce_fusion.2
  108.6 10.6 %collective-permute-done = bf16[8,2,128,128]{3,2,0,1:T(8,128)(2,1)S(1)} collective-permute-done((bf16[8,2,128,128]{3,2,0,1:T(8,128)(2,1)S(1)}, bf16[8,2,128,128]{3,2,0,1:T(8,128)(2,1)S(1)}, u32[]{:S(2)}, u32[]{:S(2)}) %collective-permute-start) | collective-permute-done | bytes 524320 | tf_op jit(solution)/shard_map/ppermute | solution.py:46
  119.2 3.7 %collective-permute-start.1 = (bf16[8,2,128,128]{3,2,0,1:T(8,128)(2,1)S(1)}, bf16[8,2,128,128]{3,2,0,1:T(8,128)(2,1)S(1)}, u32[]{:S(2)}, u32[]{:S(2)}) collective-permute-start(bf16[8,2,128,128]{3,2,0,1:T(8,128)(2,1)S(1)} %collective-permute-done), channel_id=1, source_target_pairs={{0,224},{32,0},{64,32},{96,64},{128,96},{160,128},{192,160},{224,1... | collective-permute-start | bytes 1572872 | tf_op jit(solution)/shard_map/ppermute | solution.py:46
  122.9 0.2 broadcast_compare_fusion
  123.1 26.4 %collective-permute-done.4 = bf16[8,2,128,128]{3,2,0,1:T(8,128)(2,1)S(1)} collective-permute-done((bf16[8,2,128,128]{3,2,0,1:T(8,128)(2,1)S(1)}, bf16[8,2,128,128]{3,2,0,1:T(8,128)(2,1)S(1)}, u32[]{:S(2)}, u32[]{:S(2)}) %collective-permute-start.4) | collective-permute-done | bytes 524320 | tf_op jit(solution)/shard_map/ppermute | solution.py:47
  149.6 3.3 collective-permute-start.2
  153.0 22.9 %collective-permute-done.5 = bf16[8,2,128,128]{3,2,0,1:T(8,128)(2,1)S(1)} collective-permute-done((bf16[8,2,128,128]{3,2,0,1:T(8,128)(2,1)S(1)}, bf16[8,2,128,128]{3,2,0,1:T(8,128)(2,1)S(1)}, u32[]{:S(2)}, u32[]{:S(2)}) %collective-permute-start.5) | collective-permute-done | bytes 524320 | tf_op jit(solution)/shard_map/ppermute | solution.py:47
  176.0 2.0 constant_dynamic-update-slice_fusion.7
  178.0 3.5 %collective-permute-start.7 = (bf16[4,2,128,128]{3,2,0,1:T(8,128)(2,1)S(1)}, bf16[4,2,128,128]{3,2,0,1:T(8,128)(2,1)S(1)}, u32[]{:S(2)}, u32[]{:S(2)}) collective-permute-start(bf16[4,2,128,128]{3,2,0,1:T(8,128)(2,1)S(1)} %slice.73), channel_id=1, source_target_pairs={{0,224},{32,0},{64,32},{96,64},{128,96},{160,128},{192,160},{224,1... | collective-permute-start | bytes 786440 | tf_op jit(solution)/shard_map/ppermute | solution.py:53
  181.5 0.9 constant_dynamic-update-slice_fusion.6
  182.4 0.9 constant_dynamic-update-slice_fusion.5
  183.3 7.4 %collective-permute-done.6 = bf16[4,2,128,128]{3,2,0,1:T(8,128)(2,1)S(1)} collective-permute-done((bf16[4,2,128,128]{3,2,0,1:T(8,128)(2,1)S(1)}, bf16[4,2,128,128]{3,2,0,1:T(8,128)(2,1)S(1)}, u32[]{:S(2)}, u32[]{:S(2)}) %collective-permute-start.6) | collective-permute-done | bytes 262176 | tf_op jit(solution)/shard_map/ppermute | solution.py:52
  190.8 0.7 constant_dynamic-update-slice_fusion.4
  191.5 0.7 constant_dynamic-update-slice_fusion.3
  192.2 0.9 constant_dynamic-update-slice_fusion.2
  193.2 0.9 constant_dynamic-update-slice_fusion.1
  194.1 0.9 constant_dynamic-update-slice_fusion
  195.0 8.2 %gather_fusion = bf16[96,2,128,128]{3,2,1,0:T(8,128)(2,1)} fusion(bf16[64,2,128,128]{3,2,0,1:T(8,128)(2,1)} %constant_dynamic-update-slice_fusion, s32[1024]{0:T(1024)S(1)} %pad_clamp_fusion.1), kind=kCustom, calls=%fused_computation | custom fusion | bytes 12583296 | tf_op jit(solution)/shard_map/gather | solution.py:94
  203.2 4.2 %fusion.58 = (bf16[8,12,1,128,128]{4,3,2,1,0:T(8,128)(2,1)S(1)}, bf16[8,12,1,128,128]{4,3,2,1,0:T(8,128)(2,1)S(1)}) fusion(bf16[8,12,2,128,128]{4,3,2,1,0:T(8,128)(2,1)} %bitcast.107), kind=kLoop, calls=%fused_computation.110 | loop fusion | bytes 12582912 | tf_op jit(solution)/shard_map/slice | solution.py:96
  207.4 1.2 select_reduce_fusion.1
  208.6 0.5 copy-done.3
  209.0 1.5 select_reduce_fusion
  210.5 1.7 fusion.31
  212.2 7.4 %fusion.27 = bf16[8,1,128,128]{3,2,0,1:T(8,128)(2,1)S(1)} fusion(bf16[8,1536,128]{2,1,0:T(8,128)(2,1)} %bitcast.113, f32[8,128,1536]{2,1,0:T(8,128)} %copy-done.2, bf16[8,128,128]{2,1,0:T(8,128)(2,1)S(1)} %bitcast.130, bf16[8,1536,128]{2,1,0:T(8,128)(2,1)} %bitcast.124, f32[8,128]{1,0:T(8,128)S(1)} %get-tuple-element.20, f32[8,128]{1,0:T(8,128)S(1)} %log_add_fusion, ...), kind=kOutput, calls=%fused_computation.32 | convolution fusion | flops 815005696 | bytes 13127680 | tf_op jit(solution)/shard_map/sab,sbd->sad/dot_general | solution.py:116
  219.7 4.2 %all_to_all.73 = bf16[8,2,128,1,128]{4,2,1,3,0:T(8,128)(2,1)S(1)} all-to-all(bf16[8,2,128,1,128]{4,2,1,3,0:T(8,128)(2,1)S(1)} %copy.68), channel_id=1, replica_groups=mesh['z'=8,'core'=2,'tp'=16] {'core'}, dimensions={0} | all-to-all | bytes 1048576 | tf_op jit(solution)/shard_map/all_to_all | solution.py:31
  223.9 0.5 copy.93
  224.4 0.4 fusion.60
  224.8 5.4 %convolution_bitcast_fusion = f32[4096,256]{0,1:T(8,128)} fusion(bf16[512,4096]{1,0:T(8,128)(2,1)} %bitcast.13, bf16[64,8,2,128]{3,2,1,0:T(2,128)(2,1)S(1)} %bitcast.128), kind=kOutput, calls=%fused_computation.9 | convolution fusion | flops 1073741824 | bytes 8650752 | tf_op jit(solution)/shard_map/dot_general | solution.py:162
  230.2 6.6 %reshape.274 = f32[8,2,256,256]{2,1,0,3:T(2,128)} reshape(f32[4096,256]{0,1:T(8,128)} %convolution_bitcast_fusion) | data formatting | bytes 8388608 | tf_op jit(solution)/shard_map/reshape | solution.py:167
  236.8 7.2 %copy.76 = f32[8,2,256,256]{3,2,0,1:T(8,128)} copy(f32[8,2,256,256]{2,1,0,3:T(2,128)} %reshape.274) | data formatting | bytes 8388608 | tf_op jit(solution)/shard_map/reshape | solution.py:167
  244.5 0.3 select_reduce_fusion.3
  245.0 0.3 fusion.38
  245.4 0.9 reshape_squeeze.25
  246.2 24.6 %all_gather.7 = f32[64,2,128]{2,1,0:T(2,128)S(1)} all-gather(f32[8,2,128]{2,1,0:T(2,128)S(1)} %pad_maximum_fusion.2), channel_id=1, replica_groups=mesh['z'=8,'core'=2,'tp'=16] {'z'}, dimensions={0}, use_global_device_ids=true | all-gather | bytes 73728 | tf_op jit(solution)/shard_map/all_gather | solution.py:121
  270.8 0.7 gather_fusion.2
  271.5 0.2 slice_reduce_fusion
  271.9 8.2 %gather_fusion.1 = bf16[96,2,128,128]{3,2,1,0:T(8,128)(2,1)} fusion(bf16[64,2,128,128]{3,2,0,1:T(8,128)(2,1)} %all-gather.2.cloned.1.call-done, s32[1024]{0:T(1024)S(1)} %pad_clamp_fusion), kind=kCustom, calls=%fused_computation.1 | custom fusion | bytes 12583296 | tf_op jit(solution)/shard_map/gather | solution.py:134
  280.0 8.1 %fusion.57 = (bf16[8,12,1,128,128]{4,3,2,1,0:T(8,128)(2,1)}, bf16[8,12,1,128,128]{4,3,2,1,0:T(8,128)(2,1)}) fusion(bf16[8,12,2,128,128]{4,3,2,1,0:T(8,128)(2,1)} %bitcast.108), kind=kLoop, calls=%fused_computation.109 | loop fusion | bytes 12582912 | tf_op jit(solution)/shard_map/slice | solution.py:135
  288.1 2.7 convert_element_type.57
  290.9 3.0 fusion.34
  293.9 1.3 fusion.28
  295.2 1.3 copy-done.4
  296.5 7.5 %fusion.26 = bf16[8,1,128,128]{3,2,0,1:T(8,128)(2,1)S(1)} fusion(bf16[8,1536,128]{2,1,0:T(8,128)(2,1)} %bitcast.111, f32[8,128,1536]{2,1,0:T(8,128)} %copy-done.4, bf16[8,1536,128]{2,1,0:T(8,128)(2,1)} %bitcast.121, f32[8,1536]{1,0:T(8,128)S(1)} %get-tuple-element.24, f32[8,1536]{1,0:T(8,128)S(1)} %get-tuple-element.25, ...), kind=kOutput, calls=%fused_computation.31 | convolution fusion | flops 815005696 | bytes 13217792 | tf_op jit(solution)/shard_map/tba,tad->tbd/dot_general | solution.py:151
  304.1 4.2 %all_to_all.74 = bf16[8,2,128,1,128]{4,2,1,3,0:T(8,128)(2,1)S(1)} all-to-all(bf16[8,2,128,1,128]{4,2,1,3,0:T(8,128)(2,1)S(1)} %copy.73), channel_id=1, replica_groups=mesh['z'=8,'core'=2,'tp'=16] {'core'}, dimensions={0} | all-to-all | bytes 1048576 | tf_op jit(solution)/shard_map/all_to_all | solution.py:31
  308.3 0.3 copy.74
  308.6 0.9 reshape_squeeze.28
  309.5 0.3 copy.75
  309.7 0.9 reshape_squeeze.29
  310.6 21.9 %reduce-scatter.5.cloned.1.call-done = bf16[256,256]{1,0:T(8,128)(2,1)} async-done(((bf16[2048,256]{1,0:T(8,128)(2,1)}), bf16[256,256]{1,0:T(8,128)(2,1)}) %reduce-scatter.5.cloned.1.call-update) | async-done | bytes 131088 | tf_op jit(solution)/shard_map/reduce_scatter | solution.py:169
  (69 shorter events, 2.0 us)
Async XLA Ops:
  8.0 84.3 %copy-start = (bf16[4096,256]{1,0:T(8,128)(2,1)S(1)}, bf16[4096,256]{1,0:T(8,128)(2,1)}, u32[]{:S(2)}) copy-start(bf16[4096,256]{1,0:T(8,128)(2,1)} %param.12) | copy-start | bytes 6291460
  24.2 68.1 %all-to-all-start.1 = ((bf16[16,32,4096]{2,1,0:T(8,128)(2,1)}), bf16[16,32,4096]{2,1,0:T(8,128)(2,1)}, u32[]{:S(2)}, u32[]{:S(2)}) async-start(bf16[16,32,4096]{2,1,0:T(8,128)(2,1)} %stack.24), calls=%async_computation.1 | async-start | bytes 8388608 | tf_op jit(solution)/shard_map/all_to_all | solution.py:69
  31.6 240.2 %all-gather.2.cloned.1.call-start = ((), (), s32[]{:S(2)}) async-start(), calls=%async_computation.7 | async-start | bytes 4718592 | tf_op jit(solution)/shard_map/all_gather | solution.py:120
  95.7 12.0 %copy-start.8 = (s32[64]{0:T(128)S(1)}, s32[64]{0:T(128)}, u32[]{:S(2)}) copy-start(s32[64]{0:T(128)} %param.15) | copy-start | bytes 772
  95.7 11.9 %copy-start.9 = (s32[64,12]{0,1:T(8,128)S(1)}, s32[64,12]{0,1:T(8,128)}, u32[]{:S(2)}) copy-start(s32[64,12]{0,1:T(8,128)} %param.13) | copy-start | bytes 9220
  95.8 27.2 %copy-start.10 = (s32[64,12]{0,1:T(8,128)S(1)}, s32[64,12]{0,1:T(8,128)}, u32[]{:S(2)}) copy-start(s32[64,12]{0,1:T(8,128)} %param.14) | copy-start | bytes 9220
  100.7 187.4 %reduce-scatter.3.cloned.1.call-start = ((), (), s32[]{:S(2)}) async-start(), calls=%async_computation.8 | async-start | bytes 6291456 | tf_op jit(solution)/shard_map/reduce_scatter | solution.py:168
  101.8 17.4 %collective-permute-start = (bf16[8,2,128,128]{3,2,0,1:T(8,128)(2,1)S(1)}, bf16[8,2,128,128]{3,2,0,1:T(8,128)(2,1)S(1)}, u32[]{:S(2)}, u32[]{:S(2)}) collective-permute-start(bf16[8,2,128,128]{3,2,0,1:T(8,128)(2,1)S(1)} %get-tuple-element.10), channel_id=1, source_target_pairs={{0,224},{32,0},{64,32},{96,64},{128,96},{160,128},{192,160},{224,1... | collective-permute-start | bytes 1572872 | tf_op jit(solution)/shard_map/ppermute | solution.py:46
  107.7 15.2 %collective-permute-start.3 = (bf16[8,2,128,128]{3,2,0,1:T(8,128)(2,1)S(1)}, bf16[8,2,128,128]{3,2,0,1:T(8,128)(2,1)S(1)}, u32[]{:S(2)}, u32[]{:S(2)}) collective-permute-start(bf16[8,2,128,128]{3,2,0,1:T(8,128)(2,1)S(1)} %get-tuple-element.10), channel_id=1, source_target_pairs={{0,32},{32,64},{64,96},{96,128},{128,160},{160,192},{192,224},{224... | collective-permute-start | bytes 1572872 | tf_op jit(solution)/shard_map/ppermute | solution.py:47
  119.2 30.4 %copy-start.7 = (bf16[8,2,128,128]{3,2,0,1:T(8,128)(2,1)}, bf16[8,2,128,128]{3,2,0,1:T(8,128)(2,1)S(1)}, u32[]{:S(2)}) copy-start(bf16[8,2,128,128]{3,2,0,1:T(8,128)(2,1)S(1)} %collective-permute-done) | copy-start | bytes 1572868
  119.2 30.4 %collective-permute-start.1 = (bf16[8,2,128,128]{3,2,0,1:T(8,128)(2,1)S(1)}, bf16[8,2,128,128]{3,2,0,1:T(8,128)(2,1)S(1)}, u32[]{:S(2)}, u32[]{:S(2)}) collective-permute-start(bf16[8,2,128,128]{3,2,0,1:T(8,128)(2,1)S(1)} %collective-permute-done), channel_id=1, source_target_pairs={{0,224},{32,0},{64,32},{96,64},{128,96},{160,128},{192,160},{224,1... | collective-permute-start | bytes 1572872 | tf_op jit(solution)/shard_map/ppermute | solution.py:46
  122.9 26.6 %collective-permute-start.4 = (bf16[8,2,128,128]{3,2,0,1:T(8,128)(2,1)S(1)}, bf16[8,2,128,128]{3,2,0,1:T(8,128)(2,1)S(1)}, u32[]{:S(2)}, u32[]{:S(2)}) collective-permute-start(bf16[8,2,128,128]{3,2,0,1:T(8,128)(2,1)S(1)} %collective-permute-done.3), channel_id=1, source_target_pairs={{0,32},{32,64},{64,96},{96,128},{128,160},{160,192},{192,224},{224... | collective-permute-start | bytes 1572872 | tf_op jit(solution)/shard_map/ppermute | solution.py:47
  149.5 26.4 %collective-permute-start.5 = (bf16[8,2,128,128]{3,2,0,1:T(8,128)(2,1)S(1)}, bf16[8,2,128,128]{3,2,0,1:T(8,128)(2,1)S(1)}, u32[]{:S(2)}, u32[]{:S(2)}) collective-permute-start(bf16[8,2,128,128]{3,2,0,1:T(8,128)(2,1)S(1)} %collective-permute-done.4), channel_id=1, source_target_pairs={{0,32},{32,64},{64,96},{96,128},{128,160},{160,192},{192,224},{224... | collective-permute-start | bytes 1572872 | tf_op jit(solution)/shard_map/ppermute | solution.py:47
  149.6 28.4 %collective-permute-start.2 = (bf16[8,2,128,128]{3,2,0,1:T(8,128)(2,1)S(1)}, bf16[8,2,128,128]{3,2,0,1:T(8,128)(2,1)S(1)}, u32[]{:S(2)}, u32[]{:S(2)}) collective-permute-start(bf16[8,2,128,128]{3,2,0,1:T(8,128)(2,1)S(1)} %collective-permute-done.1), channel_id=1, source_target_pairs={{0,224},{32,0},{64,32},{96,64},{128,96},{160,128},{192,160},{224,1... | collective-permute-start | bytes 1572872 | tf_op jit(solution)/shard_map/ppermute | solution.py:46
  175.9 14.8 %collective-permute-start.6 = (bf16[4,2,128,128]{3,2,0,1:T(8,128)(2,1)S(1)}, bf16[4,2,128,128]{3,2,0,1:T(8,128)(2,1)S(1)}, u32[]{:S(2)}, u32[]{:S(2)}) collective-permute-start(bf16[4,2,128,128]{3,2,0,1:T(8,128)(2,1)S(1)} %slice.72), channel_id=1, source_target_pairs={{0,32},{32,64},{64,96},{96,128},{128,160},{160,192},{192,224},{224... | collective-permute-start | bytes 786440 | tf_op jit(solution)/shard_map/ppermute | solution.py:52
  178.0 13.5 %collective-permute-start.7 = (bf16[4,2,128,128]{3,2,0,1:T(8,128)(2,1)S(1)}, bf16[4,2,128,128]{3,2,0,1:T(8,128)(2,1)S(1)}, u32[]{:S(2)}, u32[]{:S(2)}) collective-permute-start(bf16[4,2,128,128]{3,2,0,1:T(8,128)(2,1)S(1)} %slice.73), channel_id=1, source_target_pairs={{0,224},{32,0},{64,32},{96,64},{128,96},{160,128},{192,160},{224,1... | collective-permute-start | bytes 786440 | tf_op jit(solution)/shard_map/ppermute | solution.py:53
  207.4 1.6 copy-start.3
  207.4 3.1 copy-start.6
  209.0 3.2 copy-start.2
  244.1 88.4 %reduce-scatter.5.cloned.1.call-start = ((), (), s32[]{:S(2)}) async-start(), calls=%async_computation.9 | async-start | bytes 1179648 | tf_op jit(solution)/shard_map/reduce_scatter | solution.py:169
  290.8 3.0 copy-start.5
  293.9 2.6 copy-start.4
  296.5 36.0 %copy-start.1 = (bf16[4096,256]{1,0:T(8,128)(2,1)S(1)}, bf16[4096,256]{1,0:T(8,128)(2,1)}, u32[]{:S(2)}) copy-start(bf16[4096,256]{1,0:T(8,128)(2,1)} %param.12) | copy-start | bytes 6291460
Sparse Core Ops, SparseCore 0:
  100.8 90.5 all-gather.1
  291.0 41.4 reduce-scatter.4
Sparse Core Ops, SparseCore 1:
  244.2 19.9 reduce-scatter.2
